TPU v7x, 256 devices: a whole 4x4x8 slice. The times are simulated.
256 devices in a mesh: req: 64 (over z, y_lo, x), tp: 4 (over y_hi, core).
Axes of the slice: x: 4, y: 4 (y_hi: 2, y_lo: 2; y = y_hi * 2 + y_lo), z: 8, core: 2. Of those that a mesh axis runs over, the one named last changes fastest.
Arguments:
- hidden: bfloat16 [32768, 4096], P(('req', 'tp')), may hold values from -6 to 6
- norm_gain: bfloat16 [4096], replicated, may hold values from 0.099609375 to 1.8984375
- w_qkv: bfloat16 [4096, 3072], P('req', 'tp'), may hold values from -0.09375 to 0.09375
- w_out: bfloat16 [2048, 4096], P('tp', 'req'), may hold values from -0.125 to 0.125
- lengths: int32 [256], replicated, may hold values from 1 to 3072, as said below
- deal: int32 [256], replicated, may hold values from 0 to 255, as said below
- pages: int32 [256, 24], P('req'), may hold values from 0 to 95, as said below
- pool: bfloat16 [6144, 128, 1024], P('req', None, 'tp'), may hold values from -360 to 360
Outputs:
- attn_out: bfloat16 [32768, 4096], P(('req', 'tp'))
- new_kv: bfloat16 [32768, 1024], P('req', 'tp')
Inputs may be any that keep to these rules, and one draw needn't show every extreme that they name: `lengths`: at least one request has exactly 3072 cached tokens. `deal`: a permutation of the requests. `pages`: the 4 rows of one req index together hold each page number of its pool block once.
All inputs are finite; a program needn't handle non-finite values.
Results may differ from a plain program's by a relative error of at most 0.01.
The roundings to bfloat16 on the way count: a program that leaves them out, or rounds other values in their place, can miss the bound.
Values may be sent and summed in bfloat16 or wider, within the bound.
No kernel may reach another device: no remote copies, remote signals or barrier semaphores. Data moves between devices by JAX's collectives and lax.ppermute only.
A program may use at most 128 MiB of HBM per device.

v0:
```python
import math
import jax
import jax.numpy as jnp
from jax import lax
from jax.sharding import PartitionSpec as P

HEAD = 128
QH = 16
KVH = 4
PAGE = 128
NEW = 128


def rotate(values, position):
    half = values.shape[-1] // 2
    freqs = 500000.0 ** (-(jnp.arange(half, dtype=jnp.float32) * 2.0 / values.shape[-1]))
    angles = position.astype(jnp.float32)[:, None] * freqs[None, :]
    target = (angles.shape[0],) + (1,) * (values.ndim - 2) + (half,)
    cosine = jnp.cos(angles).reshape(target)
    sine = jnp.sin(angles).reshape(target)
    former = values[..., :half]
    latter = values[..., half:]
    return jnp.concatenate([former * cosine - latter * sine, latter * cosine + former * sine], -1)


def fresh_scores_of(query_matrix, recent_key_rows, score_scale):
    scores = (
        jnp.einsum(
            "eksv,qkv->kseq", query_matrix, recent_key_rows, preferred_element_type=jnp.float32
        )
        * score_scale
    )
    count_new = query_matrix.shape[0]
    causal = jnp.arange(count_new)[:, None] >= jnp.arange(count_new)[None, :]
    return jnp.where(causal, scores, -jnp.inf)


def value_weighted_rows(weights, values, form):
    return jnp.einsum(
        form, weights.astype(jnp.bfloat16), values, preferred_element_type=jnp.float32
    )


def padded_attention(
    query_matrix, recent_key_rows, recent_value_rows, pool_view, page_row, length, score_scale
):
    heads_here = pool_view.shape[2]
    cache = pool_view[page_row].reshape(-1, heads_here, 2, HEAD)
    span = cache.shape[0]
    cached_scores = (
        jnp.einsum(
            "nhgd,khd->hgnk", query_matrix, cache[:, :, 0], preferred_element_type=jnp.float32
        )
        * score_scale
    )
    cached_scores = jnp.where(jnp.arange(span, dtype=jnp.int32) < length, cached_scores, -jnp.inf)
    recent_score_rows = fresh_scores_of(query_matrix, recent_key_rows, score_scale)
    row_max = jnp.maximum(cached_scores.max(-1), recent_score_rows.max(-1))[..., None]
    cached_exp = jnp.exp(cached_scores - row_max)
    recent_exponent = jnp.exp(recent_score_rows - row_max)
    total = cached_exp.sum(-1) + recent_exponent.sum(-1)
    summed_total = value_weighted_rows(cached_exp, cache[:, :, 1], "hgnk,khd->hgnd")
    summed_total = summed_total + value_weighted_rows(
        recent_exponent, recent_value_rows, "tvqa,ats->tvqs"
    )
    return summed_total / total[..., None]


def per_device(hidden, norm_gain, w_qkv, w_out, lengths, deal, pages, pool):
    states = hidden.astype(jnp.float32)
    mean_square = jnp.mean(states * states, axis=1, keepdims=True)
    normed = (states * lax.rsqrt(mean_square + 1e-05) * norm_gain.astype(jnp.float32)).astype(
        jnp.bfloat16
    )
    gathered = lax.all_gather(normed, "tp", axis=0, tiled=True)
    tok_rows = gathered.shape[0]
    projected = jnp.dot(
        gathered,
        lax.all_gather(w_qkv, "req", axis=0, tiled=True),
        preferred_element_type=jnp.float32,
    ).astype(jnp.bfloat16)
    full_out = lax.all_gather(w_out, "req", axis=1, tiled=True)
    group = QH // KVH
    heads_here = w_qkv.shape[1] // ((group + 2) * HEAD)
    slot_count = tok_rows // NEW
    slot_ids = lax.axis_index("req") * slot_count + jnp.arange(slot_count, dtype=jnp.int32)
    slot_length = lengths[deal[slot_ids]]
    position = jnp.repeat(slot_length, NEW) + jnp.tile(jnp.arange(NEW, dtype=jnp.int32), slot_count)
    projected = projected.reshape(tok_rows, heads_here, group + 2, HEAD)
    queries = rotate(projected[:, :, :group].astype(jnp.float32), position).astype(jnp.bfloat16)
    keys_new = rotate(projected[:, :, group].astype(jnp.float32), position).astype(jnp.bfloat16)
    values_new = projected[:, :, group + 1]
    new_kv = jnp.stack([keys_new, values_new], 2).reshape(tok_rows, heads_here * 2 * HEAD)
    pool_view = pool.reshape(pool.shape[0], PAGE, heads_here, 2, HEAD)
    score_scale = 1.0 / math.sqrt(HEAD)

    def attend(local_slot):
        begin = local_slot * NEW
        query_matrix = lax.dynamic_slice_in_dim(queries, begin, NEW, 0)
        recent_key_rows = lax.dynamic_slice_in_dim(keys_new, begin, NEW, 0)
        recent_value_rows = lax.dynamic_slice_in_dim(values_new, begin, NEW, 0)
        page_row = pages[local_slot]
        length = slot_length[local_slot]
        result = padded_attention(
            query_matrix,
            recent_key_rows,
            recent_value_rows,
            pool_view,
            page_row,
            length,
            score_scale,
        )
        result = result.astype(jnp.bfloat16)
        return result.transpose(2, 0, 1, 3).reshape(NEW, heads_here * group * HEAD)

    contexts = lax.map(attend, jnp.arange(slot_count, dtype=jnp.int32))
    context = contexts.reshape(tok_rows, heads_here * group * HEAD)
    attn_out = lax.psum_scatter(
        jnp.dot(context, full_out, preferred_element_type=jnp.float32).astype(jnp.bfloat16),
        "tp",
        scatter_dimension=0,
        tiled=True,
    )
    return (attn_out, new_kv)


def solution(mesh):
    in_specs = (
        P(("req", "tp"), None),
        P(),
        P("req", "tp"),
        P("tp", "req"),
        P(),
        P(),
        P("req", None),
        P("req", None, "tp"),
    )
    out_specs = (P(("req", "tp"), None), P("req", "tp"))
    return jax.shard_map(
        per_device, mesh=mesh, in_specs=in_specs, out_specs=out_specs, check_vma=False
    )
```

profile of v0, /device:TPU:1, one launch (start us, length us, event | category | flops | bytes accessed | tf_op | source)
XLA Modules:
  0.0 734.8 jit_solution(14359055821439632575)
XLA Ops:
  7.2 0.7 convert_element_type.81
  7.9 1.5 fusion.32
  9.5 2.5 fusion.34
  12.1 0.7 all-gather.6.cloned.1.call-update
  12.8 0.7 all-gather.8.cloned.1.call-update
  13.6 0.6 gather_fusion.1
  14.3 0.6 gather_fusion.2
  15.0 9.7 %reshape.408 = bf16[96,128,1,2,128]{4,3,2,1,0:T(2,128)(2,1)} reshape(bf16[96,128,256]{2,1,0:T(8,128)(2,1)} %param.17) | data formatting | bytes 12582912 | tf_op jit(solution)/shard_map/reshape | solution.py:94
  25.3 32.2 %all-gather.4.cloned.1.call-done = bf16[512,4096]{1,0:T(8,128)(2,1)} async-done(((bf16[128,4096]{1,0:T(8,128)(2,1)}), bf16[512,4096]{1,0:T(8,128)(2,1)}) %all-gather.4.cloned.1.call-update) | async-done | bytes 4194320 | tf_op jit(solution)/shard_map/all_gather | solution.py:75
  57.4 262.9 %all-gather.6.cloned.1.call-done = bf16[4096,768]{1,0:T(8,128)(2,1)} async-done(((bf16[64,768]{1,0:T(8,128)(2,1)}), bf16[4096,768]{1,0:T(8,128)(2,1)}) %all-gather.6.cloned.1.call-update) | async-done | bytes 6291472 | tf_op jit(solution)/shard_map/all_gather | solution.py:79
  320.4 7.5 %convolution_convert_fusion.1 = bf16[512,768]{1,0:T(8,128)(2,1)S(1)} fusion(bf16[512,4096]{1,0:T(8,128)(2,1)} %all-gather.4.cloned.1.call-done, bf16[4096,768]{1,0:T(8,128)(2,1)} %all-gather.6.cloned.1.call-done), kind=kOutput, calls=%fused_computation.53 | convolution fusion | flops 3221618688 | bytes 11272192 | tf_op jit(solution)/shard_map/dot_general | solution.py:77
  329.1 76.6 %while.10 = (s32[]{:T(128)}, bf16[4,128,512]{2,1,0:T(8,128)(2,1)S(1)}, s32[4]{0:T(128)S(1)}, s32[4]{0:T(128)S(1)}, s32[4,24]{1,0:T(4,128)}, /*index=5*/bf16[96,1...) while((s32[]{:T(128)}, ...), condition=%wide.region_6.7_spmd, body=%wide.region_1.6_spmd.sunk | while | flops 856837184 | bytes 29113984 | solution.py:116
  329.1 0.6 dynamic_slice.60
  332.3 0.7 fusion.64
  333.0 8.2 %gather_fusion = bf16[24,128,2,128]{3,2,1,0:T(2,128)(2,1)S(1)} fusion(bf16[96,128,2,128]{3,2,1,0:T(2,128)(2,1)} %bitcast.156, s32[1024]{0:T(1024)S(1)} %pad_clamp_fusion.4), kind=kCustom, calls=%fused_computation.clone.1 | custom fusion | bytes 3145824 | tf_op jit(solution)/shard_map/while/body/eval_jaxpr/gather | solution.py:48
  341.6 0.6 dynamic_slice.61
  342.2 0.7 iota_compare_fusion.4
  342.8 1.0 bitcast_reduce_fusion.2
  344.2 2.0 fusion.67
  346.2 1.7 fusion.66
  348.3 0.6 dynamic_slice.60
  351.4 0.7 fusion.64
  352.1 8.2 %gather_fusion = bf16[24,128,2,128]{3,2,1,0:T(2,128)(2,1)S(1)} fusion(bf16[96,128,2,128]{3,2,1,0:T(2,128)(2,1)} %bitcast.156, s32[1024]{0:T(1024)S(1)} %pad_clamp_fusion.4), kind=kCustom, calls=%fused_computation.clone.1 | custom fusion | bytes 3145824 | tf_op jit(solution)/shard_map/while/body/eval_jaxpr/gather | solution.py:48
  360.7 0.6 dynamic_slice.61
  361.3 0.7 iota_compare_fusion.4
  362.0 1.0 bitcast_reduce_fusion.2
  363.3 2.0 fusion.67
  365.3 1.7 fusion.66
  367.4 0.6 dynamic_slice.60
  370.6 0.7 fusion.64
  371.3 8.2 %gather_fusion = bf16[24,128,2,128]{3,2,1,0:T(2,128)(2,1)S(1)} fusion(bf16[96,128,2,128]{3,2,1,0:T(2,128)(2,1)} %bitcast.156, s32[1024]{0:T(1024)S(1)} %pad_clamp_fusion.4), kind=kCustom, calls=%fused_computation.clone.1 | custom fusion | bytes 3145824 | tf_op jit(solution)/shard_map/while/body/eval_jaxpr/gather | solution.py:48
  379.9 0.6 dynamic_slice.61
  380.5 0.7 iota_compare_fusion.4
  381.1 1.0 bitcast_reduce_fusion.2
  382.4 2.0 fusion.67
  384.4 1.7 fusion.66
  386.5 0.6 dynamic_slice.60
  389.7 0.7 fusion.64
  390.4 8.2 %gather_fusion = bf16[24,128,2,128]{3,2,1,0:T(2,128)(2,1)S(1)} fusion(bf16[96,128,2,128]{3,2,1,0:T(2,128)(2,1)} %bitcast.156, s32[1024]{0:T(1024)S(1)} %pad_clamp_fusion.4), kind=kCustom, calls=%fused_computation.clone.1 | custom fusion | bytes 3145824 | tf_op jit(solution)/shard_map/while/body/eval_jaxpr/gather | solution.py:48
  399.0 0.6 dynamic_slice.61
  399.6 0.7 iota_compare_fusion.4
  400.3 1.0 bitcast_reduce_fusion.2
  401.6 2.0 fusion.67
  403.6 1.7 fusion.66
  405.7 216.2 %all-gather.8.cloned.1.call-done = bf16[512,4096]{0,1:T(8,128)(2,1)} async-done(((bf16[512,64]{0,1:T(8,128)(2,1)}), bf16[512,4096]{0,1:T(8,128)(2,1)}) %all-gather.8.cloned.1.call-update) | async-done | bytes 4194320 | tf_op jit(solution)/shard_map/all_gather | solution.py:82
  621.9 6.5 convolution_convert_fusion
  628.5 0.8 copy.27
  629.3 98.9 %reduce-scatter.2.cloned.1.call-done = bf16[128,4096]{1,0:T(8,128)(2,1)} async-done(((bf16[512,4096]{1,0:T(8,128)(2,1)}), bf16[128,4096]{1,0:T(8,128)(2,1)}) %reduce-scatter.2.cloned.1.call-update) | async-done | bytes 1048592 | tf_op jit(solution)/shard_map/reduce_scatter | solution.py:118
  (68 shorter events, 6.3 us)
Async XLA Ops:
  7.2 6.4 copy-start
  7.2 7.1 copy-start.1
  7.2 50.2 %all-gather.4.cloned.1.call-start = ((), (), s32[]{:S(2)}) async-start(), calls=%async_computation.1 | async-start | bytes 5242880 | tf_op jit(solution)/shard_map/all_gather | solution.py:75
  12.0 308.3 %all-gather.6.cloned.1.call-start = ((), (), s32[]{:S(2)}) async-start(), calls=%async_computation.2 | async-start | bytes 6389760 | tf_op jit(solution)/shard_map/all_gather | solution.py:79
  12.8 609.2 %all-gather.8.cloned.1.call-start = ((), (), s32[]{:S(2)}) async-start(), calls=%async_computation.3 | async-start | bytes 4259840 | tf_op jit(solution)/shard_map/all_gather | solution.py:82
  13.5 714.7 %reduce-scatter.2.cloned.1.call-start = ((), (), s32[]{:S(2)}) async-start(), calls=%async_computation.4 | async-start | bytes 5242880 | tf_op jit(solution)/shard_map/reduce_scatter | solution.py:118
Sparse Core Ops, SparseCore 0:
  12.1 45.2 all-gather.3
  59.2 261.0 all-gather.5
  322.1 299.7 all-gather.7
  628.6 99.5 reduce-scatter.1
where the time goes:
time: 736 us; the launch traced here: 735 us
  waiting for transfers between devices  612 us (83%)
  local copies, waits for them, and re-layouts  51.7 us (7%)
  matrix products  26.6 us (4%)
  other arithmetic  20 us (3%)
  between operations  13.9 us (2%)
  loops' own time  10.8 us (1%)
    all_gather x1, waiting for transfers between devices, per_device(): lax.all_gather(w_qkv, 'req', axis=0, tiled=True)  263 us
    all_gather x1, waiting for transfers between devices, per_device(): full_out = lax.all_gather(w_out, 'req', axis=1, tiled=True)  216 us
    reduce_scatter x1, waiting for transfers between devices, per_device(): lax.psum_scatter(jnp.dot(context, full_out, preferred_element_type=jnp.fl...  98.9 us
    gather x8, local copies, waits for them, and re-layouts, padded_attention(): cache = pool_view[page_row].reshape(-1, heads_here, 2, HEAD)  34.3 us
    all_gather x1, waiting for transfers between devices, per_device(): gathered = lax.all_gather(normed, 'tp', axis=0, tiled=True)  32.2 us
  transfers between devices with their start and end apart: 4, of which 4 were waited for; matrix products, arithmetic and copies ran while one was open for 12% of the time, Pallas kernels for 0%

commit v1 on v0

--- a/solution.py
+++ b/solution.py
@@ -79,7 +79,9 @@
         lax.all_gather(w_qkv, "req", axis=0, tiled=True),
         preferred_element_type=jnp.float32,
     ).astype(jnp.bfloat16)
-    full_out = lax.all_gather(w_out, "req", axis=1, tiled=True)
+    full_out = jnp.concatenate(
+        lax.all_to_all(jnp.stack([w_out] * lax.axis_size("req")), "req", 0, 0), axis=1
+    )
     group = QH // KVH
     heads_here = w_qkv.shape[1] // ((group + 2) * HEAD)
     slot_count = tok_rows // NEW

time: 736 us -> 553 us (0.75)
  waiting for transfers between devices: 612 us -> 413 us
  starting transfers between devices: 0.16 us -> 13.9 us
    all_gather x1 -> x0, waiting for transfers between devices: 216 us -> none  [per_device(): full_out = lax.all_gather(w_out, 'req', axis=1, tiled=True)]
    all_to_all x0 -> x1, starting transfers between devices: none -> 13.8 us  [per_device(): lax.all_to_all(jnp.stack([w_out] * lax.axis_size('req')), 'req', 0, 0)]
    all_gather x1, waiting for transfers between devices: 32.2 us -> 45.7 us  [per_device(): gathered = lax.all_gather(normed, 'tp', axis=0, tiled=True)]
  transfers between devices with their start and end apart: 4 -> 4, of which waited for: 4 -> 3; matrix products, arithmetic and copies ran while one was open for 12% -> 16% of each run, Pallas kernels for 0% -> 0%
where the time goes in v1:
time: 553 us; the launch traced here: 552 us
  waiting for transfers between devices  413 us (75%)
  local copies, waits for them, and re-layouts  54.3 us (10%)
  matrix products  26.6 us (5%)
  other arithmetic  20 us (4%)
  starting transfers between devices  13.9 us (3%)
  between operations  13.9 us (3%)
  loops' own time  10.8 us (2%)
    all_gather x1, waiting for transfers between devices, per_device(): lax.all_gather(w_qkv, 'req', axis=0, tiled=True)  270 us
    reduce_scatter x1, waiting for transfers between devices, per_device(): lax.psum_scatter(jnp.dot(context, full_out, preferred_element_type=jnp.fl...  96.6 us
    all_gather x1, waiting for transfers between devices, per_device(): gathered = lax.all_gather(normed, 'tp', axis=0, tiled=True)  45.7 us
    gather x8, local copies, waits for them, and re-layouts, padded_attention(): cache = pool_view[page_row].reshape(-1, heads_here, 2, HEAD)  34.3 us
    all_to_all x1, starting transfers between devices, per_device(): lax.all_to_all(jnp.stack([w_out] * lax.axis_size('req')), 'req', 0, 0)  13.8 us
  transfers between devices with their start and end apart: 4, of which 3 were waited for; matrix products, arithmetic and copies ran while one was open for 16% of the time, Pallas kernels for 0%

profile of v1, /device:TPU:1, one launch (start us, length us, event | category | flops | bytes accessed | tf_op | source)
XLA Modules:
  0.0 552.1 jit_solution(7508195321610588339)
XLA Ops:
  7.2 0.7 convert_element_type.81
  7.9 1.5 fusion.32
  9.5 2.5 fusion.34
  12.1 0.7 all-gather.5.cloned.1.call-update
  12.8 2.4 stack.4
  15.2 13.8 %all-to-all-start = ((bf16[64,512,64]{1,2,0:T(8,128)(2,1)}), bf16[64,512,64]{1,2,0:T(8,128)(2,1)}, u32[]{:S(2)}, u32[]{:S(2)}) async-start(bf16[64,512,64]{1,2,0:T(8,128)(2,1)} %stack.4), calls=%async_computation | async-start | bytes 8388608 | tf_op jit(solution)/shard_map/all_to_all | solution.py:83
  29.1 9.9 %reshape.416 = bf16[96,128,1,2,128]{4,3,2,1,0:T(2,128)(2,1)} reshape(bf16[96,128,256]{2,1,0:T(8,128)(2,1)} %param.17) | data formatting | bytes 12582912 | tf_op jit(solution)/shard_map/reshape | solution.py:96
  38.9 0.6 gather_fusion.1
  39.6 0.6 gather_fusion.2
  40.9 45.7 %all-gather.3.cloned.1.call-done = bf16[512,4096]{1,0:T(8,128)(2,1)} async-done(((bf16[128,4096]{1,0:T(8,128)(2,1)}), bf16[512,4096]{1,0:T(8,128)(2,1)}) %all-gather.3.cloned.1.call-update) | async-done | bytes 4194320 | tf_op jit(solution)/shard_map/all_gather | solution.py:75
  86.5 269.7 %all-gather.5.cloned.1.call-done = bf16[4096,768]{1,0:T(8,128)(2,1)} async-done(((bf16[64,768]{1,0:T(8,128)(2,1)}), bf16[4096,768]{1,0:T(8,128)(2,1)}) %all-gather.5.cloned.1.call-update) | async-done | bytes 6291472 | tf_op jit(solution)/shard_map/all_gather | solution.py:79
  356.2 7.5 %convolution_convert_fusion.1 = bf16[512,768]{1,0:T(8,128)(2,1)S(1)} fusion(bf16[512,4096]{1,0:T(8,128)(2,1)} %all-gather.3.cloned.1.call-done, bf16[4096,768]{1,0:T(8,128)(2,1)} %all-gather.5.cloned.1.call-done), kind=kOutput, calls=%fused_computation.53 | convolution fusion | flops 3221618688 | bytes 11272192 | tf_op jit(solution)/shard_map/dot_general | solution.py:77
  365.0 76.6 %while.10 = (s32[]{:T(128)}, bf16[4,128,512]{2,1,0:T(8,128)(2,1)S(1)}, s32[4]{0:T(128)S(1)}, s32[4]{0:T(128)S(1)}, s32[4,24]{1,0:T(4,128)}, /*index=5*/bf16[96,1...) while((s32[]{:T(128)}, ...), condition=%wide.region_6.7_spmd, body=%wide.region_1.6_spmd.sunk | while | flops 856837184 | bytes 29113984 | solution.py:118
  365.0 0.6 dynamic_slice.60
  368.2 0.7 fusion.64
  368.9 8.2 %gather_fusion = bf16[24,128,2,128]{3,2,1,0:T(2,128)(2,1)S(1)} fusion(bf16[96,128,2,128]{3,2,1,0:T(2,128)(2,1)} %bitcast.159, s32[1024]{0:T(1024)S(1)} %pad_clamp_fusion.4), kind=kCustom, calls=%fused_computation.clone.1 | custom fusion | bytes 3145824 | tf_op jit(solution)/shard_map/while/body/eval_jaxpr/gather | solution.py:48
  377.5 0.6 dynamic_slice.61
  378.1 0.7 iota_compare_fusion.4
  378.7 1.0 bitcast_reduce_fusion.2
  380.1 2.0 fusion.67
  382.1 1.7 fusion.66
  384.2 0.6 dynamic_slice.60
  387.3 0.7 fusion.64
  388.0 8.2 %gather_fusion = bf16[24,128,2,128]{3,2,1,0:T(2,128)(2,1)S(1)} fusion(bf16[96,128,2,128]{3,2,1,0:T(2,128)(2,1)} %bitcast.159, s32[1024]{0:T(1024)S(1)} %pad_clamp_fusion.4), kind=kCustom, calls=%fused_computation.clone.1 | custom fusion | bytes 3145824 | tf_op jit(solution)/shard_map/while/body/eval_jaxpr/gather | solution.py:48
  396.6 0.6 dynamic_slice.61
  397.2 0.7 iota_compare_fusion.4
  397.9 1.0 bitcast_reduce_fusion.2
  399.2 2.0 fusion.67
  401.2 1.7 fusion.66
  403.3 0.6 dynamic_slice.60
  406.5 0.7 fusion.64
  407.2 8.2 %gather_fusion = bf16[24,128,2,128]{3,2,1,0:T(2,128)(2,1)S(1)} fusion(bf16[96,128,2,128]{3,2,1,0:T(2,128)(2,1)} %bitcast.159, s32[1024]{0:T(1024)S(1)} %pad_clamp_fusion.4), kind=kCustom, calls=%fused_computation.clone.1 | custom fusion | bytes 3145824 | tf_op jit(solution)/shard_map/while/body/eval_jaxpr/gather | solution.py:48
  415.8 0.6 dynamic_slice.61
  416.4 0.7 iota_compare_fusion.4
  417.0 1.0 bitcast_reduce_fusion.2
  418.3 2.0 fusion.67
  420.3 1.7 fusion.66
  422.4 0.6 dynamic_slice.60
  425.6 0.7 fusion.64
  426.3 8.2 %gather_fusion = bf16[24,128,2,128]{3,2,1,0:T(2,128)(2,1)S(1)} fusion(bf16[96,128,2,128]{3,2,1,0:T(2,128)(2,1)} %bitcast.159, s32[1024]{0:T(1024)S(1)} %pad_clamp_fusion.4), kind=kCustom, calls=%fused_computation.clone.1 | custom fusion | bytes 3145824 | tf_op jit(solution)/shard_map/while/body/eval_jaxpr/gather | solution.py:48
  434.9 0.6 dynamic_slice.61
  435.5 0.7 iota_compare_fusion.4
  436.2 1.0 bitcast_reduce_fusion.2
  437.5 2.0 fusion.67
  439.5 1.7 fusion.66
  441.6 6.5 %convolution_convert_fusion = bf16[512,4096]{1,0:T(8,128)(2,1)} fusion(bf16[512,512]{1,0:T(8,128)(2,1)S(1)} %bitcast.166, bf16[512,4096]{0,1:T(8,128)(2,1)} %bitcast.34), kind=kOutput, calls=%fused_computation.47 | convolution fusion | flops 2149580800 | bytes 8912896 | tf_op jit(solution)/shard_map/dot_general | solution.py:121
  448.1 0.8 copy.28
  449.0 96.6 %reduce-scatter.2.cloned.1.call-done = bf16[128,4096]{1,0:T(8,128)(2,1)} async-done(((bf16[512,4096]{1,0:T(8,128)(2,1)}), bf16[128,4096]{1,0:T(8,128)(2,1)}) %reduce-scatter.2.cloned.1.call-update) | async-done | bytes 1048592 | tf_op jit(solution)/shard_map/reduce_scatter | solution.py:120
  (70 shorter events, 6.2 us)
Async XLA Ops:
  7.2 31.8 %copy-start = (s32[256]{0:T(256)S(1)}, s32[256]{0:T(256)}, u32[]{:S(2)}) copy-start(s32[256]{0:T(256)} %param.15) | copy-start | bytes 3076
  7.2 5.6 %copy-start.2 = (bf16[512,64]{0,1:T(8,128)(2,1)S(1)}, bf16[512,64]{0,1:T(8,128)(2,1)}, u32[]{:S(2)}) copy-start(bf16[512,64]{0,1:T(8,128)(2,1)} %param.13) | copy-start | bytes 196612
  7.2 79.3 %all-gather.3.cloned.1.call-start = ((), (), s32[]{:S(2)}) async-start(), calls=%async_computation.2 | async-start | bytes 5242880 | tf_op jit(solution)/shard_map/all_gather | solution.py:75
  12.0 344.2 %all-gather.5.cloned.1.call-start = ((), (), s32[]{:S(2)}) async-start(), calls=%async_computation.3 | async-start | bytes 6389760 | tf_op jit(solution)/shard_map/all_gather | solution.py:79
  15.2 426.3 %all-to-all-start = ((bf16[64,512,64]{1,2,0:T(8,128)(2,1)}), bf16[64,512,64]{1,2,0:T(8,128)(2,1)}, u32[]{:S(2)}, u32[]{:S(2)}) async-start(bf16[64,512,64]{1,2,0:T(8,128)(2,1)} %stack.4), calls=%async_computation | async-start | bytes 8388608 | tf_op jit(solution)/shard_map/all_to_all | solution.py:83
  29.0 516.6 %reduce-scatter.2.cloned.1.call-start = ((), (), s32[]{:S(2)}) async-start(), calls=%async_computation.4 | async-start | bytes 5242880 | tf_op jit(solution)/shard_map/reduce_scatter | solution.py:120
  29.0 10.6 %copy-start.1 = (s32[256]{0:T(256)S(1)}, s32[256]{0:T(256)}, u32[]{:S(2)}) copy-start(s32[256]{0:T(256)} %param.14) | copy-start | bytes 3076
Sparse Core Ops, SparseCore 0:
  12.1 74.3 all-gather.2
  88.3 267.8 all-gather.4
  448.2 97.2 reduce-scatter.1
